TPU v7x, 256 devices: a whole 4x4x8 slice. The times are simulated.
256 devices in a mesh: tm: 2 (over core), tile: 128 (over x, z, y).
Axes of the slice: x: 4, y: 4, z: 8, core: 2. Of those that a mesh axis runs over, the one named last changes fastest.
Arguments:
- features: bfloat16 [4, 128, 128, 384], P('tm', 'tile'), may hold values from -48 to 48
- query_weight: bfloat16 [384, 384], replicated, may hold values from -1 to 1
- key_weight: bfloat16 [384, 384], replicated, may hold values from -12 to 12
- value_weight: bfloat16 [384, 384], replicated, may hold values from -0.3125 to 0.3125
- out_weight: bfloat16 [384, 384], replicated, may hold values from -1.25 to 1.25
- conv_weight: bfloat16 [3, 3, 3, 384, 384], replicated, may hold values from -0.0625 to 0.0625
Outputs:
- decoded: bfloat16 [4, 128, 128, 384], P('tm', 'tile')
All inputs are finite; a program needn't handle non-finite values.
Results may differ from a plain program's by a relative error of at most 0.019.
Values may be sent and summed in bfloat16 or wider, within the bound.
No kernel may reach another device: no remote copies, remote signals or barrier semaphores. Data moves between devices by JAX's collectives and lax.ppermute only.
A program may use at most 128 MiB of HBM per device.

v0:
```python
import math
import jax
import jax.numpy as jnp
from jax import lax
from jax.sharding import Mesh
from jax.sharding import PartitionSpec as P

ROW_AXES = ("x", "z", "y")


def rms_rows(values):
    return values * lax.rsqrt(jnp.mean(values * values, axis=-1, keepdims=True) + 1e-06)


def project(flat_rows, weight):
    return jnp.dot(flat_rows, weight, preferred_element_type=jnp.float32).astype(jnp.bfloat16)


def row_shift(block, forward):
    count = 1
    for name in ROW_AXES:
        count *= lax.axis_size(name)
    if forward:
        route = [(i, i + 1) for i in range(count - 1)]
    else:
        route = [(i + 1, i) for i in range(count - 1)]
    return lax.ppermute(block, ROW_AXES, route)


def per_device(features, query_weight, key_weight, value_weight, out_weight, conv_weight):
    frames, rows, cols, width = features.shape
    count = rows * cols
    widened = features.astype(jnp.float32)
    normed = rms_rows(widened).astype(jnp.bfloat16)
    flat = normed.reshape(frames * count, width)
    scale = 1.0 / math.sqrt(width)
    query = project(flat, query_weight).reshape(frames, count, width)
    query_all = lax.all_gather(query, "z", axis=1, tiled=True)
    normed_all = lax.all_gather(
        normed.reshape(frames, count, width), ("x", "y"), axis=1, tiled=True
    )
    keys_in = normed_all.reshape(-1, width)
    key_rows = project(keys_in, key_weight).reshape(frames, -1, width)
    value_rows = project(keys_in, value_weight).reshape(frames, -1, width)
    scores = (
        jnp.einsum("fqd,fkd->fqk", query_all, key_rows, preferred_element_type=jnp.float32) * scale
    )
    highest = lax.pmax(jnp.max(scores, axis=-1), "z")
    expo = jnp.exp(scores - highest[..., None])
    total = jnp.sum(expo, axis=-1)
    probs = expo.astype(jnp.bfloat16)
    summed = jnp.einsum("fqk,fkd->fqd", probs, value_rows, preferred_element_type=jnp.float32)
    summed = lax.psum_scatter(summed.astype(jnp.bfloat16), "z", scatter_dimension=1, tiled=True)
    total = lax.psum_scatter(total, "z", scatter_dimension=1, tiled=True)
    attended = (summed.astype(jnp.float32) / total[:, :, None]).astype(jnp.bfloat16)
    projected = jnp.dot(attended.reshape(-1, width), out_weight, preferred_element_type=jnp.float32)
    mixed = (widened + projected.reshape(features.shape)).astype(jnp.bfloat16)
    mixed_wide = mixed.astype(jnp.float32)
    activated = jax.nn.silu(rms_rows(mixed_wide)).astype(jnp.bfloat16)
    earlier = lax.ppermute(activated, "tm", [(0, 1)])
    stacked = jnp.concatenate([earlier, activated], axis=0)
    above = row_shift(stacked, True)
    below = row_shift(stacked, False)
    padded = jnp.concatenate([above, stacked, below], axis=1)
    padded = jnp.pad(padded, ((0, 0), (0, 0), (1, 1), (0, 0)))
    patches = []
    for tap_time in range(3):
        for tap_row in range(3):
            for tap_col in range(3):
                patches.append(
                    padded[
                        tap_time : tap_time + frames,
                        tap_row : tap_row + rows,
                        tap_col : tap_col + cols,
                    ]
                )
    columns = jnp.concatenate(patches, axis=-1).reshape(frames * count, 27 * width)
    conv = jnp.dot(
        columns, conv_weight.reshape(27 * width, width), preferred_element_type=jnp.float32
    )
    return (mixed_wide + conv.reshape(features.shape)).astype(jnp.bfloat16)


def solution(mesh):
    sizes = dict(zip(mesh.axis_names, mesh.devices.shape))
    tile = sizes["tile"]
    y = 4
    z = 8
    x = tile // (y * z)
    fine = Mesh(mesh.devices.reshape(sizes["tm"], x, z, y), ("tm", *ROW_AXES))
    spec = P("tm", ROW_AXES, None, None)
    in_specs = (spec, P(), P(), P(), P(), P())
    return jax.shard_map(per_device, mesh=fine, in_specs=in_specs, out_specs=spec, check_vma=False)
```

profile of v0, /device:TPU:6, one launch (start us, length us, event | category | flops | bytes accessed | tf_op | source)
XLA Modules:
  0.0 259.3 jit_solution(6664018388497770649)
XLA Ops:
  6.5 0.0 copy-start
  6.5 0.0 all-gather.6.cloned.1.call-start
  6.5 1.1 fusion.30
  7.6 1.7 fusion.31
  9.3 0.0 all-gather.6.cloned.1.call-update
  9.4 0.0 all-gather.4.cloned.1.call-start
  9.4 2.0 convolution_convert_fusion.2
  11.4 0.0 all-gather.4.cloned.1.call-update
  11.5 0.0 reduce-scatter.7.cloned.1.call-start
  11.5 53.0 %all-gather.6.cloned.1.call-done = bf16[2,1,2048,384]{3,2,0,1:T(8,128)(2,1)} async-done(((bf16[2,1,128,384]{3,2,0,1:T(8,128)(2,1)}), bf16[2,1,2048,384]{3,2,0,1:T(8,128)(2,1)}) %all-gather.6.cloned.1.call-update) | async-done | bytes 3145744 | tf_op jit(solution)/shard_map/all_gather | solution.py:39
  64.5 0.0 copy-done
  64.5 5.7 %convolution_convert_fusion = bf16[4096,384]{1,0:T(8,128)(2,1)} fusion(bf16[4096,384]{1,0:T(8,128)(2,1)} %bitcast.58, bf16[384,384]{1,0:T(8,128)(2,1)S(1)} %copy-done), kind=kOutput, calls=%fused_computation.7 | convolution fusion | flops 1209532416 | bytes 6586368 | tf_op jit(solution)/shard_map/dot_general | solution.py:16
  70.3 0.0 copy-done.1
  70.3 2.1 convolution_convert_fusion.1
  72.4 33.3 %all-gather.4.cloned.1.call-done = bf16[2,1024,384]{2,1,0:T(8,128)(2,1)} async-done(((bf16[2,128,384]{2,1,0:T(8,128)(2,1)}), bf16[2,1024,384]{2,1,0:T(8,128)(2,1)}) %all-gather.4.cloned.1.call-update) | async-done | bytes 1572880 | tf_op jit(solution)/shard_map/all_gather | solution.py:38
  105.7 9.6 %multiply_reduce_fusion = (f32[2,1024]{1,0:T(2,128)S(1)}, f32[2,1024,2048]{2,1,0:T(8,128)}) fusion(bf16[2,1024,384]{2,1,0:T(8,128)(2,1)} %all-gather.4.cloned.1.call-done, bf16[2,2048,384]{2,1,0:T(8,128)(2,1)S(1)} %bitcast.60), kind=kOutput, calls=%fused_computation.1 | convolution fusion | flops 3229612032 | bytes 21504000 | tf_op jit(solution)/shard_map/fqd,fkd->fqk/dot_general | solution.py:46
  115.3 16.1 %pmax.7 = f32[2,1024]{1,0:T(2,128)S(1)} all-reduce(f32[2,1024]{1,0:T(2,128)S(1)} %get-tuple-element.5), channel_id=1, replica_groups=mesh['tm'=2,'x'=4,'z'=8,'y'=4] {'z'}, use_global_device_ids=true, to_apply=%region_2.0 | all-reduce | flops 2048 | bytes 16384 | tf_op jit(solution)/shard_map/pmax | solution.py:48
  131.4 7.7 %fusion = f32[2,1024]{1,0:T(2,128)S(1)} fusion(f32[2,1024,2048]{2,1,0:T(8,128)} %get-tuple-element.6, f32[2,1024]{1,0:T(2,128)S(1)} %pmax.7), kind=kLoop, calls=%fused_computation.2 | loop fusion | flops 12580864 | bytes 16793600 | tf_op jit(solution)/shard_map/reduce_sum | solution.py:50
  139.1 1.0 copy.11
  140.1 0.0 reduce-scatter.7.cloned.1.call-update
  140.2 0.2 reduce-scatter.5.cloned.1.call-start
  140.4 11.5 %fusion.9 = bf16[2,1024,384]{2,1,0:T(8,128)(2,1)} fusion(bf16[2,2048,384]{2,1,0:T(8,128)(2,1)S(1)} %bitcast.61, f32[2,1024,2048]{2,1,0:T(8,128)} %get-tuple-element.6, f32[2,1024]{1,0:T(2,128)S(1)} %pmax.7), kind=kOutput, calls=%fused_computation.14 | convolution fusion | flops 3234594816 | bytes 21504000 | tf_op jit(solution)/shard_map/fqk,fkd->fqd/dot_general | solution.py:52
  151.9 0.0 reduce-scatter.5.cloned.1.call-update
  152.0 25.5 %reduce-scatter.7.cloned.1.call-done = f32[128,2]{1,0:T(8,128)} async-done(((f32[1024,2]{1,0:T(8,128)}), f32[128,2]{1,0:T(8,128)}) %reduce-scatter.7.cloned.1.call-update) | async-done | bytes 1040
  177.5 0.9 copy.12
  178.3 40.8 %reduce-scatter.5.cloned.1.call-done = bf16[2,128,384]{2,1,0:T(8,128)(2,1)} async-done(((bf16[2,1024,384]{2,1,0:T(8,128)(2,1)}), bf16[2,128,384]{2,1,0:T(8,128)(2,1)}) %reduce-scatter.5.cloned.1.call-update) | async-done | bytes 196624 | tf_op jit(solution)/shard_map/reduce_scatter | solution.py:53
  219.1 1.7 multiply_reduce_fusion.1
  220.8 0.2 multiply_convert_fusion
  221.0 1.3 collective-permute-start
  222.3 1.0 collective-permute-done
  223.4 5.8 %collective-permute-start.2 = (bf16[4,1,128,384]{3,2,0,1:T(8,128)(2,1)S(1)}, bf16[4,1,128,384]{3,2,0,1:T(8,128)(2,1)S(1)}, u32[]{:S(2)}, u32[]{:S(2)}) collective-permute-start(bf16[4,1,128,384]{3,2,0,1:T(8,128)(2,1)S(1)} %pad_maximum_fusion), channel_id=1, source_target_pairs={{1,0},{2,1},{3,2},{4,3},{5,4},{6,5},{7,6},{8,7},{9,8},{10,9},{11,1... | collective-permute-start | bytes 1179656 | tf_op jit(solution)/shard_map/ppermute | solution.py:27
  229.2 1.9 collective-permute-start.1
  231.2 7.0 %collective-permute-done.2 = bf16[4,1,128,384]{3,2,0,1:T(8,128)(2,1)S(1)} collective-permute-done((bf16[4,1,128,384]{3,2,0,1:T(8,128)(2,1)S(1)}, bf16[4,1,128,384]{3,2,0,1:T(8,128)(2,1)S(1)}, u32[]{:S(2)}, u32[]{:S(2)}) %collective-permute-start.2) | collective-permute-done | bytes 393248 | tf_op jit(solution)/shard_map/ppermute | solution.py:27
  238.1 8.3 %collective-permute-done.1 = bf16[4,1,128,384]{3,2,0,1:T(8,128)(2,1)S(1)} collective-permute-done((bf16[4,1,128,384]{3,2,0,1:T(8,128)(2,1)S(1)}, bf16[4,1,128,384]{3,2,0,1:T(8,128)(2,1)S(1)}, u32[]{:S(2)}, u32[]{:S(2)}) %collective-permute-start.1) | collective-permute-done | bytes 393248 | tf_op jit(solution)/shard_map/ppermute | solution.py:27
  246.5 0.3 select_maximum_fusion
  246.9 0.1 slice_dynamic-update-slice_fusion.21
  247.0 0.1 slice_dynamic-update-slice_fusion.19
  247.1 0.0 slice-start.1
  247.2 0.1 slice_dynamic-update-slice_fusion.16
  247.3 0.1 slice_dynamic-update-slice_fusion.13
  247.5 0.1 slice_dynamic-update-slice_fusion.11
  247.6 0.1 slice_dynamic-update-slice_fusion.8
  247.8 0.1 slice_dynamic-update-slice_fusion.5
  247.9 0.2 constant_dynamic-update-slice_fusion
  248.1 0.1 slice_dynamic-update-slice_fusion.3
  248.2 0.1 slice_dynamic-update-slice_fusion
  248.3 0.8 slice-done.1
  249.1 3.6 %fusion.27 = bf16[2,1,128,384]{3,2,1,0:T(8,128)(2,1)} fusion(f32[2,1,128,384]{3,2,0,1:T(8,128)S(1)} %get-tuple-element.8, bf16[10368,384,1]{1,0,2:T(8,128)(2,1)S(1)} %bitcast.68, bf16[2,1,128,10368]{3,2,0,1:T(8,128)(2,1)S(1)} %slice_dynamic-update-slice_fusion), kind=kOutput, calls=%fused_computation.28 | convolution fusion | flops 2038628352 | bytes 13860864 | tf_op jit(solution)/shard_map/dot_general | solution.py:78
  (28 shorter events, 0.6 us)
Async XLA Ops:
  6.5 58.0 %copy-start = (bf16[384,384]{1,0:T(8,128)(2,1)S(1)}, bf16[384,384]{1,0:T(8,128)(2,1)}, u32[]{:S(2)}) copy-start(bf16[384,384]{1,0:T(8,128)(2,1)} %param.9) | copy-start | bytes 884740
  6.5 58.0 %all-gather.6.cloned.1.call-start = ((), (), s32[]{:S(2)}) async-start(), calls=%async_computation.4 | async-start | bytes 3342336 | tf_op jit(solution)/shard_map/all_gather | solution.py:39
  9.4 96.3 %all-gather.4.cloned.1.call-start = ((), (), s32[]{:S(2)}) async-start(), calls=%async_computation.2 | async-start | bytes 1769472 | tf_op jit(solution)/shard_map/all_gather | solution.py:38
  11.5 166.0 %reduce-scatter.7.cloned.1.call-start = ((), (), s32[]{:S(2)}) async-start(), calls=%async_computation.5 | async-start | bytes 589824
  64.5 5.7 %copy-start.1 = (bf16[2,1,2048,384]{3,2,0,1:T(8,128)(2,1)S(1)}, bf16[2,1,2048,384]{3,2,0,1:T(8,128)(2,1)}, u32[]{:S(2)}) copy-start(bf16[2,1,2048,384]{3,2,0,1:T(8,128)(2,1)} %all-gather.6.cloned.1.call-done) | copy-start | bytes 9437188
  64.5 5.8 %copy-start.3 = (bf16[384,384]{1,0:T(8,128)(2,1)S(1)}, bf16[384,384]{1,0:T(8,128)(2,1)}, u32[]{:S(2)}) copy-start(bf16[384,384]{1,0:T(8,128)(2,1)} %param.8) | copy-start | bytes 884740
  131.4 9.0 %copy-start.2 = (bf16[4096,384]{1,0:T(8,128)(2,1)S(1)}, bf16[4096,384]{1,0:T(8,128)(2,1)}, u32[]{:S(2)}) copy-start(bf16[4096,384]{1,0:T(8,128)(2,1)} %convolution_convert_fusion) | copy-start | bytes 9437188
  140.2 79.0 %reduce-scatter.5.cloned.1.call-start = ((), (), s32[]{:S(2)}) async-start(), calls=%async_computation.3 | async-start | bytes 1769472 | tf_op jit(solution)/shard_map/reduce_scatter | solution.py:53
  219.1 29.2 %slice-start = ((s8[7962624]{0:T(1024)(128)(4,1)}), s8[4194304]{0:T(1024)(128)(4,1)S(1)}, s32[]{:S(2)}) async-start(s8[7962624]{0:T(1024)(128)(4,1)} %bitcast.66), calls=%async_computation.6 | async-start | bytes 8388608
  221.0 2.4 collective-permute-start
  223.4 14.7 %collective-permute-start.2 = (bf16[4,1,128,384]{3,2,0,1:T(8,128)(2,1)S(1)}, bf16[4,1,128,384]{3,2,0,1:T(8,128)(2,1)S(1)}, u32[]{:S(2)}, u32[]{:S(2)}) collective-permute-start(bf16[4,1,128,384]{3,2,0,1:T(8,128)(2,1)S(1)} %pad_maximum_fusion), channel_id=1, source_target_pairs={{1,0},{2,1},{3,2},{4,3},{5,4},{6,5},{7,6},{8,7},{9,8},{10,9},{11,1... | collective-permute-start | bytes 1179656 | tf_op jit(solution)/shard_map/ppermute | solution.py:27
  229.2 17.2 %collective-permute-start.1 = (bf16[4,1,128,384]{3,2,0,1:T(8,128)(2,1)S(1)}, bf16[4,1,128,384]{3,2,0,1:T(8,128)(2,1)S(1)}, u32[]{:S(2)}, u32[]{:S(2)}) collective-permute-start(bf16[4,1,128,384]{3,2,0,1:T(8,128)(2,1)S(1)} %pad_maximum_fusion), channel_id=1, source_target_pairs={{0,1},{1,2},{2,3},{3,4},{4,5},{5,6},{6,7},{7,8},{8,9},{9,10},{10,1... | collective-permute-start | bytes 1179656 | tf_op jit(solution)/shard_map/ppermute | solution.py:27
  247.1 2.1 slice-start.1
Sparse Core Ops, SparseCore 0:
  9.8 54.7 all-gather.5
  66.3 39.3 all-gather.3
  140.3 37.1 reduce-scatter.6
  179.9 39.2 reduce-scatter.4
where the time goes:
time: 260 us; the launch traced here: 259 us
  waiting for transfers between devices  169 us (65%)
  matrix products  36.3 us (14%)
  blocking collectives  16.1 us (6%)
  between operations  13.4 us (5%)
  other arithmetic  11.4 us (4%)
  starting transfers between devices  9.31 us (4%)
  local copies, waits for them, and re-layouts  3.88 us (1%)
    all_gather x1, waiting for transfers between devices, per_device(): lax.all_gather(normed.reshape(frames, count, width), ('x', 'y'), axis=1,...  53 us
    reduce_scatter x1, waiting for transfers between devices, per_device(): lax.psum_scatter(summed.astype(jnp.bfloat16), 'z', scatter_dimension=1, t...  40.8 us
    all_gather x1, waiting for transfers between devices, per_device(): query_all = lax.all_gather(query, 'z', axis=1, tiled=True)  33.3 us
    unnamed x5, waiting for transfers between devices  25.5 us
    pmax x1, blocking collectives, per_device(): highest = lax.pmax(jnp.max(scores, axis=-1), 'z')  16.1 us
    ppermute x2, waiting for transfers between devices, row_shift(): return lax.ppermute(block, ROW_AXES, route)  15.3 us
    dot_general x1, matrix products, per_device(): jnp.einsum('fqk,fkd->fqd', probs, value_rows, preferred_element_type=jnp....  11.5 us
    dot_general x3, matrix products, project(): jnp.dot(flat_rows, weight, preferred_element_type=jnp.float32)  9.84 us
  transfers between devices with their start and end apart: 7, of which 7 were waited for; matrix products, arithmetic and copies ran while one was open for 9% of the time, Pallas kernels for 0%

commit v1 on v0

--- a/solution.py
+++ b/solution.py
@@ -36,8 +36,14 @@
     scale = 1.0 / math.sqrt(width)
     query = project(flat, query_weight).reshape(frames, count, width)
     query_all = lax.all_gather(query, "z", axis=1, tiled=True)
-    normed_all = lax.all_gather(
-        normed.reshape(frames, count, width), ("x", "y"), axis=1, tiled=True
+    normed_all = jnp.concatenate(
+        lax.all_to_all(
+            jnp.stack([normed.reshape(frames, count, width)] * lax.axis_size(("x", "y"))),
+            ("x", "y"),
+            0,
+            0,
+        ),
+        axis=1,
     )
     keys_in = normed_all.reshape(-1, width)
     key_rows = project(keys_in, key_weight).reshape(frames, -1, width)

time: 260 us -> 224 us (0.86)
  waiting for transfers between devices: 169 us -> 121 us
  starting transfers between devices: 9.31 us -> 16.7 us
  blocking collectives: 16.1 us -> 20.2 us
    all_gather x1 -> x0, waiting for transfers between devices: 53 us -> none  [per_device(): lax.all_gather(normed.reshape(frames, count, width), ('x', 'y'), axis=1,...]
    all_to_all x0 -> x1, waiting for transfers between devices: none -> 38.7 us  [per_device(): lax.all_to_all(jnp.stack([normed.reshape(frames, count, width)] * lax.axi...]
    all_gather x1, waiting for transfers between devices: 33.3 us -> 0.02 us  [per_device(): query_all = lax.all_gather(query, 'z', axis=1, tiled=True)]
    all_to_all x0 -> x1, starting transfers between devices: none -> 7.43 us  [per_device(): lax.all_to_all(jnp.stack([normed.reshape(frames, count, width)] * lax.axi...]
    pmax x1, blocking collectives: 16.1 us -> 20.2 us  [per_device(): highest = lax.pmax(jnp.max(scores, axis=-1), 'z')]
    unnamed x5 -> x4, waiting for transfers between devices: 25.5 us -> 25.3 us
  transfers between devices with their start and end apart: 7 -> 7, of which waited for: 7 -> 6; matrix products, arithmetic and copies ran while one was open for 9% -> 10% of each run, Pallas kernels for 0% -> 0%
where the time goes in v1:
time: 224 us
  waiting for transfers between devices  121 us (54%)
  matrix products  34.1 us (15%)
  blocking collectives  20.2 us (9%)
  starting transfers between devices  16.7 us (7%)
  between operations  13.4 us (6%)
  other arithmetic  11.7 us (5%)
  local copies, waits for them, and re-layouts  6.36 us (3%)
    reduce_scatter x1, waiting for transfers between devices, per_device(): lax.psum_scatter(summed.astype(jnp.bfloat16), 'z', scatter_dimension=1, t...  40.8 us
    all_to_all x1, waiting for transfers between devices, per_device(): lax.all_to_all(jnp.stack([normed.reshape(frames, count, width)] * lax.axi...  38.7 us
    unnamed x4, waiting for transfers between devices  25.3 us
    pmax x1, blocking collectives, per_device(): highest = lax.pmax(jnp.max(scores, axis=-1), 'z')  20.2 us
    ppermute x2, waiting for transfers between devices, row_shift(): return lax.ppermute(block, ROW_AXES, route)  15.3 us
    dot_general x1, matrix products, per_device(): jnp.einsum('fqk,fkd->fqd', probs, value_rows, preferred_element_type=jnp....  11.5 us
    dot_general x1, matrix products, per_device(): jnp.einsum('fqd,fkd->fqk', query_all, key_rows, preferred_element_type=jn...  9.6 us
    reduce_sum x1, other arithmetic, per_device(): total = jnp.sum(expo, axis=-1)  7.74 us
  transfers between devices with their start and end apart: 7, of which 6 were waited for; matrix products, arithmetic and copies ran while one was open for 10% of the time, Pallas kernels for 0%

profile of v1, /device:TPU:6, one launch (start us, length us, event | category | flops | bytes accessed | tf_op | source)
XLA Modules:
  0.0 223.7 jit_solution(15122097797884886967)
XLA Ops:
  6.5 1.1 fusion.30
  7.6 1.0 fusion.47
  8.7 2.1 stack.3
  10.8 7.4 %all-to-all-start = ((bf16[16,2,128,384]{3,2,1,0:T(8,128)(2,1)}), bf16[16,2,128,384]{3,2,1,0:T(8,128)(2,1)S(1)}, u32[]{:S(2)}, u32[]{:S(2)}) async-start(bf16[16,2,128,384]{3,2,1,0:T(8,128)(2,1)} %stack.3), calls=%async_computation | async-start | bytes 6291456 | tf_op jit(solution)/shard_map/all_to_all | solution.py:40
  18.2 0.0 all-gather.2.cloned.1.call-start
  18.3 1.0 fusion.31
  19.3 1.9 convolution_convert_fusion.2
  21.2 0.0 all-gather.2.cloned.1.call-update
  21.2 0.0 reduce-scatter.7.cloned.1.call-start
  21.3 38.7 %all-to-all-done = bf16[16,2,128,384]{3,2,1,0:T(8,128)(2,1)S(1)} async-done(((bf16[16,2,128,384]{3,2,1,0:T(8,128)(2,1)}), bf16[16,2,128,384]{3,2,1,0:T(8,128)(2,1)S(1)}, u32[]{:S(2)}, u32[]{:S(2)}) %all-to-all-start) | async-done | bytes 3145760 | tf_op jit(solution)/shard_map/all_to_all | solution.py:40
  60.0 0.3 copy.12
  60.4 0.0 copy-start.2
  60.4 3.7 %convolution_convert_fusion = bf16[4096,384]{1,0:T(8,128)(2,1)} fusion(bf16[4096,384]{1,0:T(8,128)(2,1)S(1)} %bitcast.64, bf16[384,384]{1,0:T(8,128)(2,1)S(1)} %copy-done), kind=kOutput, calls=%fused_computation.7 | convolution fusion | flops 1209532416 | bytes 6586368 | tf_op jit(solution)/shard_map/dot_general | solution.py:16
  64.1 2.1 convolution_convert_fusion.1
  66.2 0.0 all-gather.2.cloned.1.call-done
  66.2 9.6 %multiply_reduce_fusion = (f32[2,1024]{1,0:T(2,128)S(1)}, f32[2,1024,2048]{2,1,0:T(8,128)}) fusion(bf16[2,1024,384]{2,1,0:T(8,128)(2,1)} %all-gather.2.cloned.1.call-done, bf16[2,2048,384]{2,1,0:T(8,128)(2,1)S(1)} %bitcast.66), kind=kOutput, calls=%fused_computation.1 | convolution fusion | flops 3229612032 | bytes 21504000 | tf_op jit(solution)/shard_map/fqd,fkd->fqk/dot_general | solution.py:52
  75.8 20.2 %pmax.7 = f32[2,1024]{1,0:T(2,128)S(1)} all-reduce(f32[2,1024]{1,0:T(2,128)S(1)} %get-tuple-element.5), channel_id=1, replica_groups=mesh['tm'=2,'x'=4,'z'=8,'y'=4] {'z'}, use_global_device_ids=true, to_apply=%region_2.0 | all-reduce | flops 2048 | bytes 16384 | tf_op jit(solution)/shard_map/pmax | solution.py:54
  96.0 7.7 %fusion = f32[2,1024]{1,0:T(2,128)S(1)} fusion(f32[2,1024,2048]{2,1,0:T(8,128)} %get-tuple-element.6, f32[2,1024]{1,0:T(2,128)S(1)} %pmax.7), kind=kLoop, calls=%fused_computation.2 | loop fusion | flops 12580864 | bytes 16793600 | tf_op jit(solution)/shard_map/reduce_sum | solution.py:56
  103.8 1.0 copy.14
  104.8 0.0 reduce-scatter.7.cloned.1.call-update
  104.8 0.2 reduce-scatter.5.cloned.1.call-start
  105.1 11.5 %fusion.9 = bf16[2,1024,384]{2,1,0:T(8,128)(2,1)} fusion(bf16[2,2048,384]{2,1,0:T(8,128)(2,1)S(1)} %bitcast.67, f32[2,1024,2048]{2,1,0:T(8,128)} %get-tuple-element.6, f32[2,1024]{1,0:T(2,128)S(1)} %pmax.7), kind=kOutput, calls=%fused_computation.14 | convolution fusion | flops 3234594816 | bytes 21504000 | tf_op jit(solution)/shard_map/fqk,fkd->fqd/dot_general | solution.py:58
  116.6 0.0 reduce-scatter.5.cloned.1.call-update
  116.6 25.3 %reduce-scatter.7.cloned.1.call-done = f32[128,2]{1,0:T(8,128)} async-done(((f32[1024,2]{1,0:T(8,128)}), f32[128,2]{1,0:T(8,128)}) %reduce-scatter.7.cloned.1.call-update) | async-done | bytes 1040
  141.9 0.9 copy.15
  142.8 40.8 %reduce-scatter.5.cloned.1.call-done = bf16[2,128,384]{2,1,0:T(8,128)(2,1)} async-done(((bf16[2,1024,384]{2,1,0:T(8,128)(2,1)}), bf16[2,128,384]{2,1,0:T(8,128)(2,1)}) %reduce-scatter.5.cloned.1.call-update) | async-done | bytes 196624 | tf_op jit(solution)/shard_map/reduce_scatter | solution.py:59
  183.6 1.7 multiply_reduce_fusion.1
  185.3 0.2 multiply_convert_fusion
  185.5 1.3 collective-permute-start
  186.8 1.0 collective-permute-done
  187.9 5.7 %collective-permute-start.2 = (bf16[4,1,128,384]{3,2,0,1:T(8,128)(2,1)S(1)}, bf16[4,1,128,384]{3,2,0,1:T(8,128)(2,1)S(1)}, u32[]{:S(2)}, u32[]{:S(2)}) collective-permute-start(bf16[4,1,128,384]{3,2,0,1:T(8,128)(2,1)S(1)} %pad_maximum_fusion), channel_id=1, source_target_pairs={{1,0},{2,1},{3,2},{4,3},{5,4},{6,5},{7,6},{8,7},{9,8},{10,9},{11,1... | collective-permute-start | bytes 1179656 | tf_op jit(solution)/shard_map/ppermute | solution.py:27
  193.7 1.9 collective-permute-start.1
  195.6 7.0 %collective-permute-done.2 = bf16[4,1,128,384]{3,2,0,1:T(8,128)(2,1)S(1)} collective-permute-done((bf16[4,1,128,384]{3,2,0,1:T(8,128)(2,1)S(1)}, bf16[4,1,128,384]{3,2,0,1:T(8,128)(2,1)S(1)}, u32[]{:S(2)}, u32[]{:S(2)}) %collective-permute-start.2) | collective-permute-done | bytes 393248 | tf_op jit(solution)/shard_map/ppermute | solution.py:27
  202.6 8.3 %collective-permute-done.1 = bf16[4,1,128,384]{3,2,0,1:T(8,128)(2,1)S(1)} collective-permute-done((bf16[4,1,128,384]{3,2,0,1:T(8,128)(2,1)S(1)}, bf16[4,1,128,384]{3,2,0,1:T(8,128)(2,1)S(1)}, u32[]{:S(2)}, u32[]{:S(2)}) %collective-permute-start.1) | collective-permute-done | bytes 393248 | tf_op jit(solution)/shard_map/ppermute | solution.py:27
  210.9 0.3 select_maximum_fusion
  211.3 0.1 slice_dynamic-update-slice_fusion.21
  211.5 0.1 slice_dynamic-update-slice_fusion.19
  211.5 0.0 slice-start.1
  211.6 0.1 slice_dynamic-update-slice_fusion.16
  211.8 0.1 slice_dynamic-update-slice_fusion.13
  211.9 0.1 slice_dynamic-update-slice_fusion.11
  212.1 0.1 slice_dynamic-update-slice_fusion.8
  212.2 0.1 slice_dynamic-update-slice_fusion.5
  212.3 0.2 constant_dynamic-update-slice_fusion
  212.5 0.1 slice_dynamic-update-slice_fusion.3
  212.7 0.1 slice_dynamic-update-slice_fusion
  212.8 0.8 slice-done.1
  213.6 3.6 %fusion.27 = bf16[2,1,128,384]{3,2,1,0:T(8,128)(2,1)} fusion(f32[2,1,128,384]{3,2,0,1:T(8,128)S(1)} %get-tuple-element.8, bf16[10368,384,1]{1,0,2:T(8,128)(2,1)S(1)} %bitcast.74, bf16[2,1,128,10368]{3,2,0,1:T(8,128)(2,1)S(1)} %slice_dynamic-update-slice_fusion), kind=kOutput, calls=%fused_computation.28 | convolution fusion | flops 2038628352 | bytes 13860864 | tf_op jit(solution)/shard_map/dot_general | solution.py:84
  (28 shorter events, 0.6 us)
Async XLA Ops:
  6.5 53.8 %copy-start = (bf16[384,384]{1,0:T(8,128)(2,1)S(1)}, bf16[384,384]{1,0:T(8,128)(2,1)}, u32[]{:S(2)}) copy-start(bf16[384,384]{1,0:T(8,128)(2,1)} %param.9) | copy-start | bytes 884740
  10.8 49.2 %all-to-all-start = ((bf16[16,2,128,384]{3,2,1,0:T(8,128)(2,1)}), bf16[16,2,128,384]{3,2,1,0:T(8,128)(2,1)S(1)}, u32[]{:S(2)}, u32[]{:S(2)}) async-start(bf16[16,2,128,384]{3,2,1,0:T(8,128)(2,1)} %stack.3), calls=%async_computation | async-start | bytes 6291456 | tf_op jit(solution)/shard_map/all_to_all | solution.py:40
  18.2 48.0 %all-gather.2.cloned.1.call-start = ((), (), s32[]{:S(2)}) async-start(), calls=%async_computation.3 | async-start | bytes 1769472 | tf_op jit(solution)/shard_map/all_gather | solution.py:38
  21.2 120.6 %reduce-scatter.7.cloned.1.call-start = ((), (), s32[]{:S(2)}) async-start(), calls=%async_computation.5 | async-start | bytes 589824
  60.4 3.7 %copy-start.2 = (bf16[384,384]{1,0:T(8,128)(2,1)S(1)}, bf16[384,384]{1,0:T(8,128)(2,1)}, u32[]{:S(2)}) copy-start(bf16[384,384]{1,0:T(8,128)(2,1)} %param.8) | copy-start | bytes 884740
  96.0 9.0 %copy-start.1 = (bf16[4096,384]{1,0:T(8,128)(2,1)S(1)}, bf16[4096,384]{1,0:T(8,128)(2,1)}, u32[]{:S(2)}) copy-start(bf16[4096,384]{1,0:T(8,128)(2,1)} %convolution_convert_fusion) | copy-start | bytes 9437188
  104.8 78.8 %reduce-scatter.5.cloned.1.call-start = ((), (), s32[]{:S(2)}) async-start(), calls=%async_computation.4 | async-start | bytes 1769472 | tf_op jit(solution)/shard_map/reduce_scatter | solution.py:59
  183.6 29.1 %slice-start = ((s8[7962624]{0:T(1024)(128)(4,1)}), s8[4194304]{0:T(1024)(128)(4,1)S(1)}, s32[]{:S(2)}) async-start(s8[7962624]{0:T(1024)(128)(4,1)} %bitcast.72), calls=%async_computation.6 | async-start | bytes 8388608
  185.5 2.4 %collective-permute-start = (bf16[2,1,128,384]{3,2,0,1:T(8,128)(2,1)S(1)}, bf16[2,1,128,384]{3,2,0,1:T(8,128)(2,1)S(1)}, u32[]{:S(2)}, u32[]{:S(2)}) collective-permute-start(bf16[2,1,128,384]{3,2,0,1:T(8,128)(2,1)S(1)} %multiply_convert_fusion), channel_id=1, source_target_pairs={{0,128},{1,129},{2,130},{3,131},{4,132},{5,133},{6,134},{7,135},{8... | collective-permute-start | bytes 589832 | tf_op jit(solution)/shard_map/ppermute | solution.py:66
  187.9 14.6 %collective-permute-start.2 = (bf16[4,1,128,384]{3,2,0,1:T(8,128)(2,1)S(1)}, bf16[4,1,128,384]{3,2,0,1:T(8,128)(2,1)S(1)}, u32[]{:S(2)}, u32[]{:S(2)}) collective-permute-start(bf16[4,1,128,384]{3,2,0,1:T(8,128)(2,1)S(1)} %pad_maximum_fusion), channel_id=1, source_target_pairs={{1,0},{2,1},{3,2},{4,3},{5,4},{6,5},{7,6},{8,7},{9,8},{10,9},{11,1... | collective-permute-start | bytes 1179656 | tf_op jit(solution)/shard_map/ppermute | solution.py:27
  193.7 17.2 %collective-permute-start.1 = (bf16[4,1,128,384]{3,2,0,1:T(8,128)(2,1)S(1)}, bf16[4,1,128,384]{3,2,0,1:T(8,128)(2,1)S(1)}, u32[]{:S(2)}, u32[]{:S(2)}) collective-permute-start(bf16[4,1,128,384]{3,2,0,1:T(8,128)(2,1)S(1)} %pad_maximum_fusion), channel_id=1, source_target_pairs={{0,1},{1,2},{2,3},{3,4},{4,5},{5,6},{6,7},{7,8},{8,9},{9,10},{10,1... | collective-permute-start | bytes 1179656 | tf_op jit(solution)/shard_map/ppermute | solution.py:27
  211.5 2.1 slice-start.1
Sparse Core Ops, SparseCore 0:
  21.4 42.3 all-gather.1
  105.0 36.8 reduce-scatter.6
  144.4 39.1 reduce-scatter.4
